TPU v7x, 256 devices: a whole 4x4x8 slice. The times are simulated.
256 devices in a mesh: row: 16 (over y, x), col: 16 (over z, core).
Axes of the slice: x: 4, y: 4, z: 8, core: 2. Of those that a mesh axis runs over, the one named last changes fastest.
Arguments:
- q_seq: bfloat16 [2048, 6144], P('row', 'col'), may hold values from -4.5 to 4.5
- k_seq: bfloat16 [2048, 6144], P('row', 'col'), may hold values from -4.5 to 4.5
- v_seq: bfloat16 [2048, 6144], P('row', 'col'), may hold values from -6 to 6
- resid: bfloat16 [2048, 6144], P('row', 'col'), may hold values from -90 to 90
- ln_gain: float32 [6144], replicated, may hold values from 0.1 to 1.9
- w_up: bfloat16 [6144, 24576], P('row', 'col'), may hold values from -0.078125 to 0.078125
Outputs:
- hidden: bfloat16 [2048, 24576], P('row', 'col')
All inputs are finite; a program needn't handle non-finite values.
Results may differ from a plain program's by a relative error of at most 0.0051.
Values may be sent and summed in bfloat16 or wider, within the bound.
No kernel may reach another device: no remote copies, remote signals or barrier semaphores. Data moves between devices by JAX's collectives and lax.ppermute only.
A program may use at most 64 MiB of HBM per device.

v0:
```python
import math
import jax
import jax.numpy as jnp
from jax import lax
from jax.sharding import Mesh, PartitionSpec as P

HD = 128


def attention_block(query, keys, values):
    seq, width = query.shape
    heads = width // HD
    qshaped = query.reshape(seq, heads, HD)
    kshaped = keys.reshape(seq, heads, HD)
    vshaped = values.reshape(seq, heads, HD)
    scores = jnp.einsum("qhd,khd->hqk", qshaped, kshaped, preferred_element_type=jnp.float32)
    scores = scores * (1.0 / math.sqrt(HD))
    rows_idx = lax.broadcasted_iota(jnp.int32, (seq, seq), 0)
    cols_idx = lax.broadcasted_iota(jnp.int32, (seq, seq), 1)
    scores = jnp.where((rows_idx >= cols_idx)[None], scores, -1e30)
    highest = jnp.max(scores, axis=-1, keepdims=True)
    expo = jnp.exp(scores - highest)
    prob = (expo / jnp.sum(expo, axis=-1, keepdims=True)).astype(jnp.bfloat16)
    output = jnp.einsum("hqk,khd->qhd", prob, vshaped, preferred_element_type=jnp.float32)
    return output.astype(jnp.bfloat16).reshape(seq, width)


def per_device(q_seq, k_seq, v_seq, resid, ln_gain, w_up):
    w_group = lax.all_gather(w_up, "rx", axis=0, tiled=True)
    res_tokens = lax.all_to_all(resid, "col", split_axis=0, concat_axis=1, tiled=True)
    attended = attention_block(q_seq, k_seq, v_seq)
    att_tokens = lax.all_to_all(attended, "col", split_axis=0, concat_axis=1, tiled=True)
    stream = res_tokens.astype(jnp.float32) + att_tokens.astype(jnp.float32)
    full_width = stream.shape[1]
    mean = jnp.sum(stream, axis=1, keepdims=True) / full_width
    spread = jnp.sum(stream * stream, axis=1, keepdims=True) / full_width - mean * mean
    normed = ((stream - mean) * lax.rsqrt(spread + 1e-05) * ln_gain[None, :]).astype(jnp.bfloat16)
    part = lax.all_to_all(normed, "ry", split_axis=1, concat_axis=0, tiled=True)
    n_y = part.shape[0] // normed.shape[0]
    part = part.reshape(n_y, normed.shape[0], part.shape[1])
    tokens = lax.all_gather(part, "col", axis=0, tiled=False)
    partial = jnp.einsum("cytf,fu->yctu", tokens, w_group, preferred_element_type=jnp.float32)
    partial = partial.reshape(-1, partial.shape[-1])
    product = lax.psum_scatter(partial, "ry", scatter_dimension=0, tiled=True)
    return jax.nn.gelu(product, approximate=True).astype(jnp.bfloat16)


def solution(mesh):
    n_row, n_col = (mesh.shape["row"], mesh.shape["col"])
    nx = len({d.coords[0] for d in mesh.devices[:, 0]})
    split = Mesh(mesh.devices.reshape(n_row // nx, nx, n_col), ("ry", "rx", "col"))
    rows = ("ry", "rx")
    placed = (P(rows, "col"), P(rows, "col"), P(rows, "col"), P(rows, "col"), P(), P(rows, "col"))

    def body(q_seq, k_seq, v_seq, resid, ln_gain, w_up):
        return per_device(q_seq, k_seq, v_seq, resid, ln_gain, w_up)

    return jax.shard_map(
        body, mesh=split, in_specs=placed, out_specs=P(rows, "col"), check_vma=False
    )
```

profile of v0, /device:TPU:1, one launch (start us, length us, event | category | flops | bytes accessed | tf_op | source)
XLA Modules:
  0.0 193.7 jit_solution(17831639695960104614)
XLA Ops:
  6.5 10.0 %all-to-all-start = ((bf16[16,8,384]{2,1,0:T(8,128)(2,1)}), bf16[16,8,384]{2,1,0:T(8,128)(2,1)S(1)}, u32[]{:S(2)}, u32[]{:S(2)}) async-start(bf16[16,8,384]{2,1,0:T(8,128)(2,1)} %bitcast.32), calls=%async_computation | async-start | bytes 196608 | tf_op jit(solution)/shard_map/all_to_all | solution.py:30
  16.5 1.0 copy.20
  17.6 1.0 copy.21
  18.6 0.2 fusion.7
  18.8 0.1 fusion.21
  18.9 1.0 copy.24
  19.9 0.3 fusion.9
  20.2 0.1 copy.27
  20.2 0.7 all_to_all.32
  21.0 4.0 %all-to-all-done = bf16[16,8,384]{2,1,0:T(8,128)(2,1)S(1)} async-done(((bf16[16,8,384]{2,1,0:T(8,128)(2,1)}), bf16[16,8,384]{2,1,0:T(8,128)(2,1)S(1)}, u32[]{:S(2)}, u32[]{:S(2)}) %all-to-all-start) | async-done | bytes 98336 | tf_op jit(solution)/shard_map/all_to_all | solution.py:30
  25.0 3.4 %all-to-all-start.1 = ((bf16[16,8,384]{2,1,0:T(8,128)(2,1)}), bf16[16,8,384]{2,1,0:T(8,128)(2,1)S(1)}, u32[]{:S(2)}, u32[]{:S(2)}) async-start(bf16[16,8,384]{2,1,0:T(8,128)(2,1)} %all_to_all.32), calls=%async_computation.1 | async-start | bytes 196608 | tf_op jit(solution)/shard_map/all_to_all | solution.py:32
  28.4 0.0 all-gather.6.cloned.1.call-start
  28.5 0.8 mul.66
  29.2 7.5 %all-to-all-done.1 = bf16[16,8,384]{2,1,0:T(8,128)(2,1)S(1)} async-done(((bf16[16,8,384]{2,1,0:T(8,128)(2,1)}), bf16[16,8,384]{2,1,0:T(8,128)(2,1)S(1)}, u32[]{:S(2)}, u32[]{:S(2)}) %all-to-all-start.1) | async-done | bytes 98336 | tf_op jit(solution)/shard_map/all_to_all | solution.py:32
  36.8 0.2 fusion.20
  37.0 0.1 multiply_convert_fusion
  37.1 8.8 %all_to_all.39 = bf16[8,4,1536]{2,0,1:T(8,128)(2,1)} all-to-all(bf16[8,4,1536]{2,0,1:T(8,128)(2,1)S(1)} %multiply_convert_fusion), channel_id=1, replica_groups=mesh['ry'=4,'rx'=4,'col'=16] {'ry'}, dimensions={1} | all-to-all | bytes 196608 | tf_op jit(solution)/shard_map/all_to_all | solution.py:38
  45.8 0.0 all-gather.6.cloned.1.call-update
  45.9 0.0 all-gather.4.cloned.1.call-start
  45.9 0.7 all-gather.4.cloned.1.call-update
  46.6 0.0 reduce-scatter.2.cloned.1.call-start
  46.7 34.7 %all-gather.6.cloned.1.call-done = bf16[64,8,1536]{2,1,0:T(8,128)(2,1)} async-done(((bf16[4,8,1536]{2,1,0:T(8,128)(2,1)}), bf16[64,8,1536]{2,1,0:T(8,128)(2,1)}) %all-gather.6.cloned.1.call-update) | async-done | bytes 1572880 | tf_op jit(solution)/shard_map/all_gather | solution.py:41
  81.4 55.2 %all-gather.4.cloned.1.call-done = bf16[1536,1536]{1,0:T(8,128)(2,1)} async-done(((bf16[384,1536]{1,0:T(8,128)(2,1)}), bf16[1536,1536]{1,0:T(8,128)(2,1)}) %all-gather.4.cloned.1.call-update) | async-done | bytes 4718608 | tf_op jit(solution)/shard_map/all_gather | solution.py:29
  136.6 4.9 %fusion.3 = f32[4,16,8,1536]{3,2,0,1:T(8,128)S(1)} fusion(bf16[16,4,8,1536]{3,2,1,0:T(8,128)(2,1)} %bitcast.34, bf16[1536,1536]{1,0:T(8,128)(2,1)} %all-gather.4.cloned.1.call-done), kind=kOutput, calls=%fused_computation.3 | convolution fusion | flops 2415919104 | bytes 9437184 | tf_op jit(solution)/shard_map/cytf,fu->yctu/dot_general | solution.py:42
  141.6 1.9 copy.28
  143.5 0.0 reduce-scatter.2.cloned.1.call-update
  143.5 41.5 %reduce-scatter.2.cloned.1.call-done = f32[128,1536]{1,0:T(8,128)} async-done(((f32[512,1536]{1,0:T(8,128)}), f32[128,1536]{1,0:T(8,128)}) %reduce-scatter.2.cloned.1.call-update) | async-done | bytes 786448 | tf_op jit(solution)/shard_map/reduce_scatter | solution.py:44
  185.0 2.1 %fusion.17 = bf16[128,1536]{1,0:T(8,128)(2,1)} fusion(f32[128,1536]{1,0:T(8,128)} %reduce-scatter.2.cloned.1.call-done), kind=kLoop, calls=%fused_computation.18 | loop fusion | flops 1769472 | bytes 1179648 | tf_op jit(solution)/shard_map/convert_element_type | solution.py:45
  (2 shorter events, 0.0 us)
Async XLA Ops:
  6.5 18.5 %all-to-all-start = ((bf16[16,8,384]{2,1,0:T(8,128)(2,1)}), bf16[16,8,384]{2,1,0:T(8,128)(2,1)S(1)}, u32[]{:S(2)}, u32[]{:S(2)}) async-start(bf16[16,8,384]{2,1,0:T(8,128)(2,1)} %bitcast.32), calls=%async_computation | async-start | bytes 196608 | tf_op jit(solution)/shard_map/all_to_all | solution.py:30
  25.0 11.8 %all-to-all-start.1 = ((bf16[16,8,384]{2,1,0:T(8,128)(2,1)}), bf16[16,8,384]{2,1,0:T(8,128)(2,1)S(1)}, u32[]{:S(2)}, u32[]{:S(2)}) async-start(bf16[16,8,384]{2,1,0:T(8,128)(2,1)} %all_to_all.32), calls=%async_computation.1 | async-start | bytes 196608 | tf_op jit(solution)/shard_map/all_to_all | solution.py:32
  28.4 53.0 %all-gather.6.cloned.1.call-start = ((), (), s32[]{:S(2)}) async-start(), calls=%async_computation.6 | async-start | bytes 1671168 | tf_op jit(solution)/shard_map/all_gather | solution.py:41
  45.9 90.8 %all-gather.4.cloned.1.call-start = ((), (), s32[]{:S(2)}) async-start(), calls=%async_computation.4 | async-start | bytes 5898240 | tf_op jit(solution)/shard_map/all_gather | solution.py:29
  46.6 138.4 %reduce-scatter.2.cloned.1.call-start = ((), (), s32[]{:S(2)}) async-start(), calls=%async_computation.5 | async-start | bytes 3932160 | tf_op jit(solution)/shard_map/reduce_scatter | solution.py:44
Sparse Core Ops, SparseCore 0:
  46.0 35.3 all-gather.5
  83.2 53.3 all-gather.3
  143.6 41.3 reduce-scatter.1
where the time goes:
time: 194 us
  waiting for transfers between devices  144 us (74%)
  starting transfers between devices  13.5 us (7%)
  between operations  13.2 us (7%)
  blocking collectives  8.75 us (5%)
  local copies, waits for them, and re-layouts  6.52 us (3%)
  matrix products  5.43 us (3%)
  other arithmetic  2.53 us (1%)
    all_gather x1, waiting for transfers between devices, per_device(): w_group = lax.all_gather(w_up, 'rx', axis=0, tiled=True)  55.2 us
    reduce_scatter x1, waiting for transfers between devices, per_device(): product = lax.psum_scatter(partial, 'ry', scatter_dimension=0, tiled=True)  41.5 us
    all_gather x1, waiting for transfers between devices, per_device(): tokens = lax.all_gather(part, 'col', axis=0, tiled=False)  34.7 us
    all_to_all x1, starting transfers between devices, per_device(): lax.all_to_all(resid, 'col', split_axis=0, concat_axis=1, tiled=True)  9.98 us
    all_to_all x1, blocking collectives, per_device(): part = lax.all_to_all(normed, 'ry', split_axis=1, concat_axis=0, tiled=True)  8.75 us
    all_to_all x1, waiting for transfers between devices, per_device(): lax.all_to_all(attended, 'col', split_axis=0, concat_axis=1, tiled=True)  7.54 us
    dot_general x1, matrix products, per_device(): jnp.einsum('cytf,fu->yctu', tokens, w_group, preferred_element_type=jnp.f...  4.94 us
    all_to_all x1, waiting for transfers between devices, per_device(): lax.all_to_all(resid, 'col', split_axis=0, concat_axis=1, tiled=True)  4.03 us
  transfers between devices with their start and end apart: 5, of which 5 were waited for; matrix products, arithmetic and copies ran while one was open for 2% of the time, Pallas kernels for 0%

commit v1 on v0

--- a/solution.py
+++ b/solution.py
@@ -26,7 +26,9 @@
 
 
 def per_device(q_seq, k_seq, v_seq, resid, ln_gain, w_up):
-    w_group = lax.all_gather(w_up, "rx", axis=0, tiled=True)
+    w_group = jnp.concatenate(
+        lax.all_to_all(jnp.stack([w_up] * lax.axis_size("rx")), "rx", 0, 0), axis=0
+    )
     res_tokens = lax.all_to_all(resid, "col", split_axis=0, concat_axis=1, tiled=True)
     attended = attention_block(q_seq, k_seq, v_seq)
     att_tokens = lax.all_to_all(attended, "col", split_axis=0, concat_axis=1, tiled=True)

time: 194 us -> 158 us (0.81)
  waiting for transfers between devices: 144 us -> 100 us
  starting transfers between devices: 13.5 us -> 18.5 us
  local copies, waits for them, and re-layouts: 6.52 us -> 9.06 us
    all_gather x1 -> x0, waiting for transfers between devices: 55.2 us -> none  [per_device(): w_group = lax.all_gather(w_up, 'rx', axis=0, tiled=True)]
    all_to_all x0 -> x1, waiting for transfers between devices: none -> 14.8 us  [per_device(): lax.all_to_all(jnp.stack([w_up] * lax.axis_size('rx')), 'rx', 0, 0)]
    reduce_scatter x1, waiting for transfers between devices: 41.5 us -> 35.5 us  [per_device(): product = lax.psum_scatter(partial, 'ry', scatter_dimension=0, tiled=True)]
    all_to_all x0 -> x1, starting transfers between devices: none -> 4.93 us  [per_device(): lax.all_to_all(jnp.stack([w_up] * lax.axis_size('rx')), 'rx', 0, 0)]
    all_gather x1, waiting for transfers between devices: 34.7 us -> 37.6 us  [per_device(): tokens = lax.all_gather(part, 'col', axis=0, tiled=False)]
    another operation x0 -> x1, local copies, waits for them, and re-layouts: none -> 2.54 us  [per_device(): jnp.stack([w_up] * lax.axis_size('rx'))]
  transfers between devices with their start and end apart: 5 -> 5, of which waited for: 5 -> 5; matrix products, arithmetic and copies ran while one was open for 2% -> 3% of each run, Pallas kernels for 0% -> 0%
where the time goes in v1:
time: 158 us
  waiting for transfers between devices  100 us (63%)
  starting transfers between devices  18.5 us (12%)
  between operations  13.5 us (9%)
  local copies, waits for them, and re-layouts  9.06 us (6%)
  blocking collectives  8.75 us (6%)
  matrix products  5.42 us (3%)
  other arithmetic  2.53 us (2%)
    all_gather x1, waiting for transfers between devices, per_device(): tokens = lax.all_gather(part, 'col', axis=0, tiled=False)  37.6 us
    reduce_scatter x1, waiting for transfers between devices, per_device(): product = lax.psum_scatter(partial, 'ry', scatter_dimension=0, tiled=True)  35.5 us
    all_to_all x1, waiting for transfers between devices, per_device(): lax.all_to_all(jnp.stack([w_up] * lax.axis_size('rx')), 'rx', 0, 0)  14.8 us
    all_to_all x1, starting transfers between devices, per_device(): lax.all_to_all(resid, 'col', split_axis=0, concat_axis=1, tiled=True)  10.1 us
    all_to_all x1, blocking collectives, per_device(): part = lax.all_to_all(normed, 'ry', split_axis=1, concat_axis=0, tiled=True)  8.75 us
    all_to_all x1, waiting for transfers between devices, per_device(): lax.all_to_all(attended, 'col', split_axis=0, concat_axis=1, tiled=True)  7.59 us
    dot_general x1, matrix products, per_device(): jnp.einsum('cytf,fu->yctu', tokens, w_group, preferred_element_type=jnp.f...  4.94 us
    all_to_all x1, starting transfers between devices, per_device(): lax.all_to_all(jnp.stack([w_up] * lax.axis_size('rx')), 'rx', 0, 0)  4.93 us
  transfers between devices with their start and end apart: 5, of which 5 were waited for; matrix products, arithmetic and copies ran while one was open for 3% of the time, Pallas kernels for 0%

profile of v1, /device:TPU:1, one launch (start us, length us, event | category | flops | bytes accessed | tf_op | source)
XLA Modules:
  0.0 157.9 jit_solution(7271602745772196043)
XLA Ops:
  6.5 0.0 copy-start
  6.5 10.1 %all-to-all-start = ((bf16[16,8,384]{2,1,0:T(8,128)(2,1)}), bf16[16,8,384]{2,1,0:T(8,128)(2,1)S(1)}, u32[]{:S(2)}, u32[]{:S(2)}) async-start(bf16[16,8,384]{2,1,0:T(8,128)(2,1)} %bitcast.31), calls=%async_computation | async-start | bytes 196608 | tf_op jit(solution)/shard_map/all_to_all | solution.py:32
  16.7 1.0 copy.20
  17.7 1.0 copy.21
  18.7 0.2 fusion.2
  18.9 0.1 fusion.16
  19.0 1.0 copy.24
  20.0 0.3 fusion.4
  20.3 0.1 copy.27
  20.4 0.7 all_to_all.35
  21.1 4.0 %all-to-all-done = bf16[16,8,384]{2,1,0:T(8,128)(2,1)S(1)} async-done(((bf16[16,8,384]{2,1,0:T(8,128)(2,1)}), bf16[16,8,384]{2,1,0:T(8,128)(2,1)S(1)}, u32[]{:S(2)}, u32[]{:S(2)}) %all-to-all-start) | async-done | bytes 98336 | tf_op jit(solution)/shard_map/all_to_all | solution.py:32
  25.1 3.4 %all-to-all-start.1 = ((bf16[16,8,384]{2,1,0:T(8,128)(2,1)}), bf16[16,8,384]{2,1,0:T(8,128)(2,1)S(1)}, u32[]{:S(2)}, u32[]{:S(2)}) async-start(bf16[16,8,384]{2,1,0:T(8,128)(2,1)} %all_to_all.35), calls=%async_computation.1 | async-start | bytes 196608 | tf_op jit(solution)/shard_map/all_to_all | solution.py:34
  28.6 0.8 mul.66
  29.3 7.6 %all-to-all-done.1 = bf16[16,8,384]{2,1,0:T(8,128)(2,1)S(1)} async-done(((bf16[16,8,384]{2,1,0:T(8,128)(2,1)}), bf16[16,8,384]{2,1,0:T(8,128)(2,1)S(1)}, u32[]{:S(2)}, u32[]{:S(2)}) %all-to-all-start.1) | async-done | bytes 98336 | tf_op jit(solution)/shard_map/all_to_all | solution.py:34
  36.9 0.2 fusion.15
  37.1 0.1 multiply_convert_fusion
  37.2 8.8 %all_to_all.44 = bf16[8,4,1536]{2,0,1:T(8,128)(2,1)} all-to-all(bf16[8,4,1536]{2,0,1:T(8,128)(2,1)S(1)} %multiply_convert_fusion), channel_id=1, replica_groups=mesh['ry'=4,'rx'=4,'col'=16] {'ry'}, dimensions={1} | all-to-all | bytes 196608 | tf_op jit(solution)/shard_map/all_to_all | solution.py:40
  46.0 0.0 copy-done
  46.0 2.5 %stack.2 = bf16[4,384,1536]{2,1,0:T(8,128)(2,1)} broadcast(bf16[384,1536]{1,0:T(8,128)(2,1)S(1)} %copy-done), dimensions={1,2} | broadcast | bytes 5898240 | tf_op jit(solution)/shard_map/stack | solution.py:30
  48.5 4.9 %all-to-all-start.3 = ((bf16[4,384,1536]{2,1,0:T(8,128)(2,1)}), bf16[4,384,1536]{2,1,0:T(8,128)(2,1)}, u32[]{:S(2)}, u32[]{:S(2)}) async-start(bf16[4,384,1536]{2,1,0:T(8,128)(2,1)} %stack.2), calls=%async_computation.3 | async-start | bytes 9437184 | tf_op jit(solution)/shard_map/all_to_all | solution.py:30
  53.4 0.0 all-gather.3.cloned.1.call-start
  53.5 0.7 all-gather.3.cloned.1.call-update
  54.2 0.0 reduce-scatter.2.cloned.1.call-start
  54.2 37.6 %all-gather.3.cloned.1.call-done = bf16[64,8,1536]{2,1,0:T(8,128)(2,1)} async-done(((bf16[4,8,1536]{2,1,0:T(8,128)(2,1)}), bf16[64,8,1536]{2,1,0:T(8,128)(2,1)}) %all-gather.3.cloned.1.call-update) | async-done | bytes 1572880 | tf_op jit(solution)/shard_map/all_gather | solution.py:43
  91.8 14.8 %all-to-all-done.3 = bf16[4,384,1536]{2,1,0:T(8,128)(2,1)} async-done(((bf16[4,384,1536]{2,1,0:T(8,128)(2,1)}), bf16[4,384,1536]{2,1,0:T(8,128)(2,1)}, u32[]{:S(2)}, u32[]{:S(2)}) %all-to-all-start.3) | async-done | bytes 4718624 | tf_op jit(solution)/shard_map/all_to_all | solution.py:30
  106.6 4.9 %convolution_bitcast_fusion = f32[4,16,8,1536]{3,2,0,1:T(8,128)S(1)} fusion(bf16[16,4,8,1536]{3,2,1,0:T(8,128)(2,1)} %bitcast.33, bf16[1536,1536,1,1]{1,0,3,2:T(8,128)(2,1)} %bitcast.11), kind=kOutput, calls=%fused_computation.1 | convolution fusion | flops 2415919104 | bytes 9437184 | tf_op jit(solution)/shard_map/cytf,fu->yctu/dot_general | solution.py:44
  111.5 1.9 %copy.28 = f32[4,16,8,1536]{3,2,1,0:T(8,128)} copy(f32[4,16,8,1536]{3,2,0,1:T(8,128)S(1)} %convolution_bitcast_fusion) | data formatting | bytes 6291456 | tf_op jit(solution)/shard_map/cytf,fu->yctu/transpose | solution.py:44
  113.4 0.0 reduce-scatter.2.cloned.1.call-update
  113.5 35.5 %reduce-scatter.2.cloned.1.call-done = f32[128,1536]{1,0:T(8,128)} async-done(((f32[512,1536]{1,0:T(8,128)}), f32[128,1536]{1,0:T(8,128)}) %reduce-scatter.2.cloned.1.call-update) | async-done | bytes 786448 | tf_op jit(solution)/shard_map/reduce_scatter | solution.py:46
  149.0 2.1 %fusion.12 = bf16[128,1536]{1,0:T(8,128)(2,1)} fusion(f32[128,1536]{1,0:T(8,128)} %reduce-scatter.2.cloned.1.call-done), kind=kLoop, calls=%fused_computation.16 | loop fusion | flops 1769472 | bytes 1179648 | tf_op jit(solution)/shard_map/convert_element_type | solution.py:47
  (2 shorter events, 0.0 us)
Async XLA Ops:
  6.5 39.4 %copy-start = (bf16[384,1536]{1,0:T(8,128)(2,1)S(1)}, bf16[384,1536]{1,0:T(8,128)(2,1)}, u32[]{:S(2)}) copy-start(bf16[384,1536]{1,0:T(8,128)(2,1)} %param.11) | copy-start | bytes 3538948
  6.5 18.6 %all-to-all-start = ((bf16[16,8,384]{2,1,0:T(8,128)(2,1)}), bf16[16,8,384]{2,1,0:T(8,128)(2,1)S(1)}, u32[]{:S(2)}, u32[]{:S(2)}) async-start(bf16[16,8,384]{2,1,0:T(8,128)(2,1)} %bitcast.31), calls=%async_computation | async-start | bytes 196608 | tf_op jit(solution)/shard_map/all_to_all | solution.py:32
  25.1 11.8 %all-to-all-start.1 = ((bf16[16,8,384]{2,1,0:T(8,128)(2,1)}), bf16[16,8,384]{2,1,0:T(8,128)(2,1)S(1)}, u32[]{:S(2)}, u32[]{:S(2)}) async-start(bf16[16,8,384]{2,1,0:T(8,128)(2,1)} %all_to_all.35), calls=%async_computation.1 | async-start | bytes 196608 | tf_op jit(solution)/shard_map/all_to_all | solution.py:34
  48.5 58.1 %all-to-all-start.3 = ((bf16[4,384,1536]{2,1,0:T(8,128)(2,1)}), bf16[4,384,1536]{2,1,0:T(8,128)(2,1)}, u32[]{:S(2)}, u32[]{:S(2)}) async-start(bf16[4,384,1536]{2,1,0:T(8,128)(2,1)} %stack.2), calls=%async_computation.3 | async-start | bytes 9437184 | tf_op jit(solution)/shard_map/all_to_all | solution.py:30
  53.4 38.3 %all-gather.3.cloned.1.call-start = ((), (), s32[]{:S(2)}) async-start(), calls=%async_computation.6 | async-start | bytes 1671168 | tf_op jit(solution)/shard_map/all_gather | solution.py:43
  54.2 94.8 %reduce-scatter.2.cloned.1.call-start = ((), (), s32[]{:S(2)}) async-start(), calls=%async_computation.5 | async-start | bytes 3932160 | tf_op jit(solution)/shard_map/reduce_scatter | solution.py:46
Sparse Core Ops, SparseCore 0:
  56.1 35.6 all-gather.2
  113.6 35.3 reduce-scatter.1
